TPU v7x, 256 devices: a whole 4x4x8 slice. The times are simulated.
256 devices in a mesh: rows: 64 (over y, z, core), freq: 4 (over x).
Axes of the slice: x: 4, y: 4, z: 8, core: 2. Of those that a mesh axis runs over, the one named last changes fastest.
Arguments:
- snapshots: bfloat16 [1048576, 512], P('rows', 'freq'), may hold values from -60 to 60
- block_cols: int32 [8192, 3], P('rows'), may hold values from 0 to 8191, as said below
- mass_blocks: bfloat16 [8192, 3, 128, 128], P('rows'), may hold values from -2 to 2
- start_group: float32 [512, 32], P('freq'), may hold values from -6 to 6
- start_merge: float32 [64, 32], replicated, may hold values from -6 to 6
Outputs:
- modes: float32 [32, 1048576], P(None, ('rows', 'freq'))
Inputs may be any that keep to these rules, and one draw needn't show every extreme that they name: block_cols[b, 0] is b; the other entries lie within 2 of b, differ from b, and may repeat near the ends.
All inputs are finite; a program needn't handle non-finite values.
Results may differ from a plain program's by a relative error of at most 0.0003.
Values may be sent and summed in bfloat16 or wider, within the bound.
No kernel may reach another device: no remote copies, remote signals or barrier semaphores. Data moves between devices by JAX's collectives and lax.ppermute only.
A program may use at most 128 MiB of HBM per device.

v0:
```python
import jax
import jax.numpy as jnp
from jax import lax
from jax.sharding import PartitionSpec as P

HB = 2
POWER = 2
HIGHEST = lax.Precision.HIGHEST


def extended_2(block, sides, width):
    for axis, dim in sides:
        count = lax.axis_size(axis)
        forward = [(i, i + 1) for i in range(count - 1)]
        backward = [(target, source) for source, target in forward]
        low = lax.ppermute(
            lax.slice_in_dim(block, block.shape[dim] - width, None, axis=dim), axis, forward
        )
        high = lax.ppermute(lax.slice_in_dim(block, 0, width, axis=dim), axis, backward)
        block = jnp.concatenate([low, block, high], axis=dim)
    return block


def orthonormal(columns_block):
    inner_gram = jnp.dot(columns_block.T, columns_block, precision=HIGHEST)
    lower_factor = jnp.linalg.cholesky(inner_gram)
    return lax.linalg.triangular_solve(
        lower_factor, columns_block, left_side=False, lower=True, transpose_a=True
    )


def subspace(gram_matrix, start_block):
    current = start_block
    for repeat in range(POWER):
        current = orthonormal(jnp.dot(gram_matrix, current, precision=HIGHEST))
    return current


def coefficient_tree(full_gram, start_merge, rank_size, freq_count):
    pairs = freq_count // 2
    width = 2 * rank_size
    blocks = jnp.stack(
        [full_gram[p * width : (p + 1) * width, p * width : (p + 1) * width] for p in range(pairs)]
    )
    pair_weights = jax.vmap(subspace, in_axes=(0, None))(blocks, start_merge)
    zero = jnp.zeros((width, rank_size), jnp.float32)
    coefficients = []
    for p in range(pairs):
        parts = [zero] * pairs
        parts[p] = pair_weights[p]
        coefficients.append(jnp.concatenate(parts, axis=0))
    while len(coefficients) > 1:
        merged = []
        for position in range(0, len(coefficients), 2):
            joined = jnp.concatenate([coefficients[position], coefficients[position + 1]], axis=1)
            pair_gram = jnp.dot(
                joined.T, jnp.dot(full_gram, joined, precision=HIGHEST), precision=HIGHEST
            )
            merged.append(jnp.dot(joined, subspace(pair_gram, start_merge), precision=HIGHEST))
        coefficients = merged
    return coefficients[0]


def shards(snapshots, block_cols, mass_blocks, start_group, start_merge):
    block_size = mass_blocks.shape[2]
    local_blocks = block_cols.shape[0]
    local_cols = snapshots.shape[1]
    total_rows = lax.axis_size("rows") * snapshots.shape[0]
    extended = extended_2(snapshots, (("rows", 0),), HB * block_size)
    tile_stack = extended.reshape(local_blocks + 2 * HB, block_size, local_cols)
    local_index = block_cols - lax.axis_index("rows") * local_blocks + HB
    picked = tile_stack[local_index]
    weighted = jnp.einsum("bkij,bkjc->bic", mass_blocks, picked, preferred_element_type=jnp.float32)
    weighted = weighted.reshape(local_blocks * block_size, local_cols)
    local_gram = jnp.dot(weighted.T, weighted, precision=HIGHEST)
    group_gram = lax.psum(local_gram, "rows") / total_rows
    weights = subspace(group_gram, start_group)
    modes = lax.dot_general(weights, weighted, (((0,), (1,)), ((), ())), precision=HIGHEST)
    rank_size = modes.shape[0]
    freq_count = lax.axis_size("freq")
    quarter = lax.all_to_all(modes, "freq", 1, 0, tiled=True)
    full_gram = (
        lax.psum(jnp.dot(quarter, quarter.T, precision=HIGHEST), ("rows", "freq")) / total_rows
    )
    combined = coefficient_tree(full_gram, start_merge, rank_size, freq_count)
    result = jnp.dot(combined.T, quarter, precision=HIGHEST)
    return result


def solution(mesh):
    in_specs = (
        P("rows", "freq"),
        P("rows", None),
        P("rows", None, None, None),
        P("freq", None),
        P(),
    )
    out_specs = P(None, ("rows", "freq"))
    return jax.shard_map(shards, mesh=mesh, in_specs=in_specs, out_specs=out_specs, check_vma=False)
```

profile of v0, /device:TPU:1, one launch (start us, length us, event | category | flops | bytes accessed | tf_op | source)
XLA Modules:
  0.0 596.8 jit_solution(17205891390755514347)
XLA Ops:
  6.5 0.9 fusion.50
  7.4 4.9 collective-permute-start
  12.4 1.9 collective-permute-start.1
  14.3 0.7 compare_select_fusion
  15.3 2.6 collective-permute-done.1
  18.0 10.8 %pad_maximum_fusion = bf16[16896,128]{1,0:T(8,128)(2,1)} fusion(bf16[256,128]{1,0:T(8,128)(2,1)S(1)} %collective-permute-done.1, bf16[16384,128]{1,0:T(8,128)(2,1)} %param.13, bf16[256,128]{1,0:T(8,128)(2,1)S(1)} %collective-permute-done), kind=kLoop, calls=%fused_computation.3 | loop fusion | flops 12976128 | bytes 8650752 | tf_op jit(solution)/shard_map/concatenate | solution.py:20
  28.7 13.6 %gather_fusion = bf16[384,128,128]{2,1,0:T(8,128)(2,1)} fusion(bf16[132,128,128]{2,1,0:T(8,128)(2,1)} %bitcast.133, s32[1024]{0:T(1024)S(1)} %pad_clamp_fusion), kind=kCustom, calls=%fused_computation | custom fusion | bytes 25167360 | tf_op jit(solution)/shard_map/gather | solution.py:72
  42.3 14.8 %fusion.62 = f32[128,128,128,1]{1,2,3,0:T(8,128)} fusion(bf16[128,3,128,128]{3,2,1,0:T(8,128)(2,1)} %param.15, bf16[128,3,128,128]{3,2,1,0:T(8,128)(2,1)} %bitcast.132), kind=kOutput, calls=%fused_computation.103 | convolution fusion | flops 1610612736 | bytes 33554432 | tf_op jit(solution)/shard_map/bkij,bkjc->bic/dot_general | solution.py:73
  57.1 17.6 %fusion.2 = f32[128,128]{1,0:T(8,128)} fusion(f32[128,128,128,1]{1,2,3,0:T(8,128)} %fusion.62), kind=kOutput, calls=%fused_computation.4 | convolution fusion | flops 3221225472 | bytes 8454144 | tf_op jit(solution)/shard_map/dot_general | solution.py:75
  74.7 173.3 %all-reduce.5.cloned.1.call-done = f32[128,128]{1,0:T(8,128)} async-done(((f32[128,128]{1,0:T(8,128)}), f32[128,128]{1,0:T(8,128)}) %all-reduce.5.cloned.1.call-update) | async-done | bytes 65552 | tf_op jit(solution)/shard_map/psum | solution.py:76
  248.0 1.0 fusion.7
  249.3 2.9 cholesky.117
  252.3 0.6 compare_reduce_fusion.5
  252.9 0.7 fusion.17
  253.6 2.4 custom-call.18
  256.0 0.2 convolution_bitcast_fusion.5
  256.3 1.0 fusion.5
  257.6 2.9 cholesky.128
  260.5 0.6 compare_reduce_fusion.4
  261.2 0.7 fusion.18
  261.8 2.4 custom-call.19
  264.3 0.2 convolution_bitcast_fusion.4
  264.5 13.0 %fusion.53 = f32[32,4,4096]{2,0,1:T(8,128)} fusion(f32[128,32,1]{0,1,2:T(8,128)S(1)} %convolution_bitcast_fusion.4, f32[4,4096,128]{2,1,0:T(8,128)} %bitcast.131), kind=kOutput, calls=%fused_computation.94 | convolution fusion | flops 805306368 | bytes 10502144 | tf_op jit(solution)/shard_map/dot_general | solution.py:78
  277.5 4.0 all-to-all-start
  281.5 25.8 %all-to-all-done = f32[32,4,4096]{2,0,1:T(8,128)S(1)} async-done(((f32[32,4,4096]{2,0,1:T(8,128)}), f32[32,4,4096]{2,0,1:T(8,128)S(1)}, u32[]{:S(2)}, u32[]{:S(2)}) %all-to-all-start) | async-done | bytes 2097184 | tf_op jit(solution)/shard_map/all_to_all | solution.py:81
  307.2 2.4 fusion.54
  309.7 237.2 %all-reduce.7.cloned.1.call-done = f32[128,128]{1,0:T(8,128)} async-done(((f32[128,128]{1,0:T(8,128)}), f32[128,128]{1,0:T(8,128)}) %all-reduce.7.cloned.1.call-update) | async-done | bytes 65552 | tf_op jit(solution)/shard_map/psum | solution.py:83
  546.9 0.8 broadcast_multiply_fusion
  547.8 0.3 fusion.10
  548.4 6.1 %custom-call.20 = f32[2,32,32]{2,1,0:T(8,128)S(1)} custom-call(f32[2,32,32]{2,1,0:T(8,128)S(1)} %fusion.14), custom_call_target="Cholesky" | custom-call | tf_op jit(solution)/shard_map/vmap(jit(cholesky))/cholesky | solution.py:26
  554.8 4.9 custom-call.21
  559.7 0.3 convolution_bitcast_fusion.1
  560.5 5.9 custom-call.22
  566.6 4.9 custom-call.23
  571.5 0.3 convolution_bitcast_fusion
  571.8 1.1 fusion.36
  572.8 0.2 fusion.35
  573.5 2.9 cholesky.161
  576.5 0.6 compare_reduce_fusion.1
  577.1 0.7 fusion.19
  577.8 2.4 custom-call.24
  580.2 0.2 convolution_bitcast_fusion.3
  580.9 2.9 cholesky.172
  583.8 0.6 compare_reduce_fusion
  584.5 0.7 fusion.20
  585.1 2.4 custom-call.25
  587.6 0.2 convolution_bitcast_fusion.2
  588.0 2.0 fusion.61
  (48 shorter events, 3.3 us)
Async XLA Ops:
  6.5 541.3 %copy-start = (f32[64,32]{0,1:T(8,128)S(1)}, f32[64,32]{0,1:T(8,128)}, u32[]{:S(2)}) copy-start(f32[64,32]{0,1:T(8,128)} %param.17) | copy-start | bytes 24580
  6.5 241.5 %all-reduce.5.cloned.1.call-start = ((), (), s32[]{:S(2)}) async-start(), calls=%async_computation.1 | async-start | bytes 131072 | tf_op jit(solution)/shard_map/psum | solution.py:76
  7.4 7.9 %collective-permute-start = (bf16[256,128]{1,0:T(8,128)(2,1)S(1)}, bf16[256,128]{1,0:T(8,128)(2,1)S(1)}, u32[]{:S(2)}, u32[]{:S(2)}) collective-permute-start(bf16[256,128]{1,0:T(8,128)(2,1)S(1)} %get-tuple-element.6), channel_id=1, source_target_pairs={{0,4},{4,8},{8,12},{12,16},{16,20},{20,24},{24,28},{28,32},{32,36}... | collective-permute-start | bytes 196616 | tf_op jit(solution)/shard_map/ppermute | solution.py:16
  12.4 5.6 collective-permute-start.1
  57.1 191.0 %copy-start.1 = (f32[128,32]{0,1:T(8,128)S(1)}, f32[128,32]{0,1:T(8,128)}, u32[]{:S(2)}) copy-start(f32[128,32]{0,1:T(8,128)} %param.16) | copy-start | bytes 49156
  277.5 29.7 %all-to-all-start = ((f32[32,4,4096]{2,0,1:T(8,128)}), f32[32,4,4096]{2,0,1:T(8,128)S(1)}, u32[]{:S(2)}, u32[]{:S(2)}) async-start(f32[32,4,4096]{2,0,1:T(8,128)} %fusion.53), calls=%async_computation | async-start | bytes 4194304 | tf_op jit(solution)/shard_map/all_to_all | solution.py:81
  281.5 265.5 %all-reduce.7.cloned.1.call-start = ((), (), s32[]{:S(2)}) async-start(), calls=%async_computation.2 | async-start | bytes 131072 | tf_op jit(solution)/shard_map/psum | solution.py:83
Sparse Core Ops, SparseCore 0:
  74.8 173.1 all-reduce.4
  309.8 237.0 all-reduce.6
where the time goes:
time: 597 us
  waiting for transfers between devices  439 us (74%)
  other arithmetic  61.4 us (10%)
  matrix products  56.6 us (9%)
  local copies, waits for them, and re-layouts  15.3 us (3%)
  between operations  13.7 us (2%)
  starting transfers between devices  10.8 us (2%)
    psum x1, waiting for transfers between devices, shards(): lax.psum(jnp.dot(quarter, quarter.T, precision=HIGHEST), ('rows', 'freq'))  237 us
    psum x1, waiting for transfers between devices, shards(): group_gram = lax.psum(local_gram, 'rows') / total_rows  173 us
    another operation x19, other arithmetic, orthonormal(): lower_factor = jnp.linalg.cholesky(inner_gram)  26.7 us
    all_to_all x1, waiting for transfers between devices, shards(): quarter = lax.all_to_all(modes, 'freq', 1, 0, tiled=True)  25.8 us
    another operation x13, other arithmetic, orthonormal(): lax.linalg.triangular_solve(lower_factor, columns_block, left_side=False,...  22.3 us
    dot_general x1, matrix products, shards(): local_gram = jnp.dot(weighted.T, weighted, precision=HIGHEST)  17.6 us
    dot_general x1, matrix products, shards(): jnp.einsum('bkij,bkjc->bic', mass_blocks, picked, preferred_element_type=...  14.8 us
    gather x1, local copies, waits for them, and re-layouts, shards(): picked = tile_stack[local_index]  13.6 us
  transfers between devices with their start and end apart: 5, of which 4 were waited for; matrix products, arithmetic and copies ran while one was open for 0% of the time, Pallas kernels for 0%

commit v1 on v0

--- a/solution.py
+++ b/solution.py
@@ -2,10 +2,16 @@
 import jax.numpy as jnp
 from jax import lax
 from jax.sharding import PartitionSpec as P
+from jax.lax import all_gather
 
 HB = 2
 POWER = 2
 HIGHEST = lax.Precision.HIGHEST
+
+
+def classes_carry(raw, along_axis):
+    r2 = all_gather(raw, along_axis)
+    return jnp.sum(r2, 0)
 
 
 def extended_2(block, sides, width):
@@ -80,7 +86,7 @@
     freq_count = lax.axis_size("freq")
     quarter = lax.all_to_all(modes, "freq", 1, 0, tiled=True)
     full_gram = (
-        lax.psum(jnp.dot(quarter, quarter.T, precision=HIGHEST), ("rows", "freq")) / total_rows
+        classes_carry(jnp.dot(quarter, quarter.T, precision=HIGHEST), ("rows", "freq")) / total_rows
     )
     combined = coefficient_tree(full_gram, start_merge, rank_size, freq_count)
     result = jnp.dot(combined.T, quarter, precision=HIGHEST)

time: 597 us -> 483 us (0.81)
  waiting for transfers between devices: 439 us -> 297 us
  blocking collectives: 0 us -> 29.2 us
    psum x1 -> x0, waiting for transfers between devices: 237 us -> none  [shards(): lax.psum(jnp.dot(quarter, quarter.T, precision=HIGHEST), ('rows', 'freq'))]
    all_gather x0 -> x1, waiting for transfers between devices: none -> 121 us  [classes_carry(): r2 = all_gather(raw, along_axis)]
    all_to_all x0 -> x1, blocking collectives: none -> 29.2 us  [shards(): quarter = lax.all_to_all(modes, 'freq', 1, 0, tiled=True)]
    all_to_all x1 -> x0, waiting for transfers between devices: 25.8 us -> none  [shards(): quarter = lax.all_to_all(modes, 'freq', 1, 0, tiled=True)]
    reduce_sum x0 -> x1, other arithmetic: none -> 6.59 us  [classes_carry(): return jnp.sum(r2, 0)]
  transfers between devices with their start and end apart: 5 -> 4, of which waited for: 4 -> 3; matrix products, arithmetic and copies ran while one was open for 0% -> 0% of each run, Pallas kernels for 0% -> 0%
where the time goes in v1:
time: 483 us
  waiting for transfers between devices  297 us (61%)
  other arithmetic  66.9 us (14%)
  matrix products  53.5 us (11%)
  blocking collectives  29.2 us (6%)
  local copies, waits for them, and re-layouts  15.3 us (3%)
  between operations  13.7 us (3%)
  starting transfers between devices  6.89 us (1%)
    psum x1, waiting for transfers between devices, shards(): group_gram = lax.psum(local_gram, 'rows') / total_rows  173 us
    all_gather x1, waiting for transfers between devices, classes_carry(): r2 = all_gather(raw, along_axis)  121 us
    all_to_all x1, blocking collectives, shards(): quarter = lax.all_to_all(modes, 'freq', 1, 0, tiled=True)  29.2 us
    another operation x19, other arithmetic, orthonormal(): lower_factor = jnp.linalg.cholesky(inner_gram)  26.4 us
    another operation x13, other arithmetic, orthonormal(): lax.linalg.triangular_solve(lower_factor, columns_block, left_side=False,...  22.3 us
    dot_general x1, matrix products, shards(): local_gram = jnp.dot(weighted.T, weighted, precision=HIGHEST)  17.6 us
    dot_general x1, matrix products, shards(): jnp.einsum('bkij,bkjc->bic', mass_blocks, picked, preferred_element_type=...  14.8 us
    gather x1, local copies, waits for them, and re-layouts, shards(): picked = tile_stack[local_index]  13.6 us
  transfers between devices with their start and end apart: 4, of which 3 were waited for; matrix products, arithmetic and copies ran while one was open for 0% of the time, Pallas kernels for 0%

profile of v1, /device:TPU:1, one launch (start us, length us, event | category | flops | bytes accessed | tf_op | source)
XLA Modules:
  0.0 482.8 jit_solution(7609455857864870101)
XLA Ops:
  6.5 0.9 fusion.50
  7.4 4.9 %collective-permute-start = (bf16[256,128]{1,0:T(8,128)(2,1)S(1)}, bf16[256,128]{1,0:T(8,128)(2,1)S(1)}, u32[]{:S(2)}, u32[]{:S(2)}) collective-permute-start(bf16[256,128]{1,0:T(8,128)(2,1)S(1)} %get-tuple-element.6), channel_id=1, source_target_pairs={{0,4},{4,8},{8,12},{12,16},{16,20},{20,24},{24,28},{28,32},{32,36}... | collective-permute-start | bytes 196616 | tf_op jit(solution)/shard_map/ppermute | solution.py:22
  12.4 1.9 collective-permute-start.1
  14.3 0.7 compare_select_fusion
  15.3 2.6 collective-permute-done.1
  18.0 10.8 %pad_maximum_fusion = bf16[16896,128]{1,0:T(8,128)(2,1)} fusion(bf16[256,128]{1,0:T(8,128)(2,1)S(1)} %collective-permute-done.1, bf16[16384,128]{1,0:T(8,128)(2,1)} %param.13, bf16[256,128]{1,0:T(8,128)(2,1)S(1)} %collective-permute-done), kind=kLoop, calls=%fused_computation.3 | loop fusion | flops 12976128 | bytes 8650752 | tf_op jit(solution)/shard_map/concatenate | solution.py:26
  28.7 13.6 %gather_fusion = bf16[384,128,128]{2,1,0:T(8,128)(2,1)} fusion(bf16[132,128,128]{2,1,0:T(8,128)(2,1)} %bitcast.134, s32[1024]{0:T(1024)S(1)} %pad_clamp_fusion), kind=kCustom, calls=%fused_computation | custom fusion | bytes 25167360 | tf_op jit(solution)/shard_map/gather | solution.py:78
  42.3 14.8 %fusion.62 = f32[128,128,128,1]{1,2,3,0:T(8,128)} fusion(bf16[128,3,128,128]{3,2,1,0:T(8,128)(2,1)} %param.15, bf16[128,3,128,128]{3,2,1,0:T(8,128)(2,1)} %bitcast.133), kind=kOutput, calls=%fused_computation.103 | convolution fusion | flops 1610612736 | bytes 33554432 | tf_op jit(solution)/shard_map/bkij,bkjc->bic/dot_general | solution.py:79
  57.1 17.6 %fusion.2 = f32[128,128]{1,0:T(8,128)} fusion(f32[128,128,128,1]{1,2,3,0:T(8,128)} %fusion.62), kind=kOutput, calls=%fused_computation.4 | convolution fusion | flops 3221225472 | bytes 8454144 | tf_op jit(solution)/shard_map/dot_general | solution.py:81
  74.7 173.3 %all-reduce.4.cloned.1.call-done = f32[128,128]{1,0:T(8,128)} async-done(((f32[128,128]{1,0:T(8,128)}), f32[128,128]{1,0:T(8,128)}) %all-reduce.4.cloned.1.call-update) | async-done | bytes 65552 | tf_op jit(solution)/shard_map/psum | solution.py:82
  248.0 1.0 fusion.7
  249.3 2.9 cholesky.117
  252.3 0.6 compare_reduce_fusion.5
  252.9 0.7 fusion.17
  253.6 2.4 custom-call.18
  256.0 0.2 convolution_bitcast_fusion.5
  256.3 1.0 fusion.5
  257.6 2.9 cholesky.128
  260.5 0.6 compare_reduce_fusion.4
  261.2 0.7 fusion.18
  261.8 2.4 custom-call.19
  264.3 0.2 convolution_bitcast_fusion.4
  264.5 10.7 %fusion.53 = f32[32,4,4096]{2,0,1:T(8,128)S(1)} fusion(f32[128,32,1]{0,1,2:T(8,128)S(1)} %convolution_bitcast_fusion.4, f32[4,4096,128]{2,1,0:T(8,128)} %bitcast.132), kind=kOutput, calls=%fused_computation.94 | convolution fusion | flops 805306368 | bytes 10502144 | tf_op jit(solution)/shard_map/dot_general | solution.py:84
  275.2 29.2 %all_to_all.16 = f32[32,4,4096]{2,0,1:T(8,128)S(1)} all-to-all(f32[32,4,4096]{2,0,1:T(8,128)S(1)} %fusion.53), channel_id=1, replica_groups=mesh['rows'=64,'freq'=4] {'freq'}, dimensions={1} | all-to-all | bytes 4194304 | tf_op jit(solution)/shard_map/all_to_all | solution.py:87
  304.4 2.4 fusion.54
  306.9 121.4 %all-gather.3.cloned.1.call-done = f32[32768,128]{1,0:T(8,128)} async-done(((f32[128,128]{1,0:T(8,128)}), f32[32768,128]{1,0:T(8,128)}) %all-gather.3.cloned.1.call-update) | async-done | bytes 16777232 | tf_op jit(solution)/shard_map/all_gather | solution.py:13
  428.3 6.6 %reduce_sum.9 = f32[128,128]{1,0:T(8,128)S(1)} reduce(f32[256,128,128]{2,1,0:T(8,128)} %bitcast.137, f32[]{:T(128)} %constant.83.clone.1), dimensions={0}, to_apply=%region_3.6 | reduce | flops 4177920 | bytes 16842756 | tf_op jit(solution)/shard_map/reduce_sum | solution.py:14
  435.0 0.3 fusion.10
  435.5 5.9 %custom-call.20 = f32[2,32,32]{2,1,0:T(8,128)S(1)} custom-call(f32[2,32,32]{2,1,0:T(8,128)S(1)} %fusion.14), custom_call_target="Cholesky" | custom-call | tf_op jit(solution)/shard_map/vmap(jit(cholesky))/cholesky | solution.py:32
  441.6 4.9 %custom-call.21 = f32[2,1,32,32]{2,3,1,0:T(8,128)S(1)} custom-call(f32[2,1,32,32]{3,2,1,0:T(8,128)S(1)} %select_bitcast_fusion.1), custom_call_target="InvertDiagBlocksLowerTriangular" | custom-call | tf_op jit(solution)/shard_map/vmap()/triangular_solve/custom-call.3 | solution.py:33
  446.5 0.3 convolution_bitcast_fusion.1
  446.8 0.2 fusion.9
  447.3 5.9 %custom-call.22 = f32[2,32,32]{2,1,0:T(8,128)S(1)} custom-call(f32[2,32,32]{2,1,0:T(8,128)S(1)} %fusion.12), custom_call_target="Cholesky" | custom-call | tf_op jit(solution)/shard_map/vmap(jit(cholesky))/cholesky | solution.py:32
  453.4 4.9 %custom-call.23 = f32[2,1,32,32]{2,3,1,0:T(8,128)S(1)} custom-call(f32[2,1,32,32]{3,2,1,0:T(8,128)S(1)} %select_bitcast_fusion), custom_call_target="InvertDiagBlocksLowerTriangular" | custom-call | tf_op jit(solution)/shard_map/vmap()/triangular_solve/custom-call.3 | solution.py:33
  458.3 0.3 convolution_bitcast_fusion
  458.6 0.2 fusion.36
  458.9 0.2 fusion.35
  459.5 2.9 cholesky.161
  462.5 0.6 compare_reduce_fusion.1
  463.1 0.7 fusion.19
  463.8 2.4 custom-call.24
  466.2 0.2 convolution_bitcast_fusion.3
  466.9 2.9 cholesky.172
  469.8 0.6 compare_reduce_fusion
  470.5 0.7 fusion.20
  471.1 2.4 custom-call.25
  473.6 0.2 convolution_bitcast_fusion.2
  474.0 2.0 fusion.61
  (48 shorter events, 3.1 us)
Async XLA Ops:
  6.5 428.4 %copy-start = (f32[64,32]{0,1:T(8,128)S(1)}, f32[64,32]{0,1:T(8,128)}, u32[]{:S(2)}) copy-start(f32[64,32]{0,1:T(8,128)} %param.17) | copy-start | bytes 24580
  6.5 241.5 %all-reduce.4.cloned.1.call-start = ((), (), s32[]{:S(2)}) async-start(), calls=%async_computation.1 | async-start | bytes 131072 | tf_op jit(solution)/shard_map/psum | solution.py:82
  7.4 7.9 %collective-permute-start = (bf16[256,128]{1,0:T(8,128)(2,1)S(1)}, bf16[256,128]{1,0:T(8,128)(2,1)S(1)}, u32[]{:S(2)}, u32[]{:S(2)}) collective-permute-start(bf16[256,128]{1,0:T(8,128)(2,1)S(1)} %get-tuple-element.6), channel_id=1, source_target_pairs={{0,4},{4,8},{8,12},{12,16},{16,20},{20,24},{24,28},{28,32},{32,36}... | collective-permute-start | bytes 196616 | tf_op jit(solution)/shard_map/ppermute | solution.py:22
  12.4 5.6 %collective-permute-start.1 = (bf16[256,128]{1,0:T(8,128)(2,1)S(1)}, bf16[256,128]{1,0:T(8,128)(2,1)S(1)}, u32[]{:S(2)}, u32[]{:S(2)}) collective-permute-start(bf16[256,128]{1,0:T(8,128)(2,1)S(1)} %get-tuple-element.8), channel_id=1, source_target_pairs={{4,0},{8,4},{12,8},{16,12},{20,16},{24,20},{28,24},{32,28},{36,32}... | collective-permute-start | bytes 196616 | tf_op jit(solution)/shard_map/ppermute | solution.py:25
  57.1 191.0 %copy-start.1 = (f32[128,32]{0,1:T(8,128)S(1)}, f32[128,32]{0,1:T(8,128)}, u32[]{:S(2)}) copy-start(f32[128,32]{0,1:T(8,128)} %param.16) | copy-start | bytes 49156
  74.7 353.6 %all-gather.3.cloned.1.call-start = ((), (), s32[]{:S(2)}) async-start(), calls=%async_computation.2 | async-start | bytes 16842752 | tf_op jit(solution)/shard_map/all_gather | solution.py:13
Sparse Core Ops, SparseCore 0:
  74.8 173.1 all-reduce.3
  307.0 121.2 all-gather.2
